TPU v7x, 512 devices: a whole 4x4x16 slice. The times are simulated.
512 devices in a mesh: row: 16 (over z), col: 4 (over x_hi, core), depth: 8 (over y, x_lo).
Axes of the slice: x: 4 (x_hi: 2, x_lo: 2; x = x_hi * 2 + x_lo), y: 4, z: 16, core: 2. Of those that a mesh axis runs over, the one named last changes fastest.
Arguments:
- ks_matrix: bfloat16 [4096, 16384], P('col', ('row', 'depth')), may hold values from -6 to 6
- sign_matrix: bfloat16 [16, 8, 128, 12288], P('col', 'depth', None, 'row'), may hold values from -0.046875 to 0.046875
- ks_mask: int32 [32, 128], P('col', ('row', 'depth')), may hold values 0 or 1
- sign_mask: int32 [16, 8, 1, 96], P('col', 'depth', None, 'row'), may hold values 0 or 1
- product_mask: int32 [32, 96], P('col', 'row'), may hold values 0 or 1
- row_order: int32 [4, 8], P('col'), may hold values from 0 to 7, each once within a row
Outputs:
- next_matrix: bfloat16 [4096, 12288], P(('col', 'depth'), 'row')
Inputs may be any that keep to these rules, and one draw needn't show every extreme that they name: Each row of row_order names every number of 0 to 7 once.
All inputs are finite; a program needn't handle non-finite values. No bound on the sum of `ks_mask` or of `sign_mask` or of `product_mask` on one device may be relied on, other than what follows from the above.
Results may differ from a plain program's by a relative error of at most 0.001.
Values may be sent and summed in bfloat16 or wider, within the bound.
No kernel may reach another device: no remote copies, remote signals or barrier semaphores. Data moves between devices by JAX's collectives and lax.ppermute only.
A program may use at most 64 MiB of HBM per device.

v0:
```python
import jax
import jax.numpy as jnp
from jax import lax
from jax.sharding import PartitionSpec as P

BS = 128


def per_device(ks_matrix, sign_matrix, ks_mask, sign_mask, product_mask, row_order):
    row_blocks, inner_blocks = ks_mask.shape
    local_groups = sign_mask.shape[0]
    sign_inner = sign_mask.shape[2]
    col_blocks = sign_mask.shape[3]
    ks_panel = (
        ks_matrix.reshape(row_blocks, BS, inner_blocks, BS)
        * ks_mask.astype(jnp.bfloat16)[:, None, :, None]
    )
    ks_panel = ks_panel.reshape(row_blocks * BS, inner_blocks * BS)
    sign_kept = sign_matrix.reshape(local_groups, sign_inner, BS, col_blocks, BS)
    sign_kept = sign_kept * sign_mask.astype(jnp.bfloat16).reshape(
        local_groups, sign_inner, 1, col_blocks, 1
    )
    sign_kept = sign_kept.reshape(local_groups, sign_inner * BS, col_blocks * BS)
    sign_whole = lax.all_gather(sign_kept, "col", axis=0, tiled=True)
    ks_whole = lax.all_gather(ks_panel, "row", axis=0, tiled=False)
    product = jnp.einsum("sik,skn->in", ks_whole, sign_whole, preferred_element_type=jnp.float32)
    filtered = (
        product.reshape(row_blocks, BS, col_blocks, BS)
        * product_mask.astype(jnp.float32)[:, None, :, None]
    )
    arranged = jnp.take(filtered, row_order[0], axis=0)
    arranged = arranged.reshape(row_blocks * BS, col_blocks * BS)
    summed = lax.psum_scatter(arranged, "depth", scatter_dimension=0, tiled=True)
    return summed.astype(jnp.bfloat16)


def solution(mesh):
    in_specs = (
        P("col", ("row", "depth")),
        P("col", "depth", None, "row"),
        P("col", ("row", "depth")),
        P("col", "depth", None, "row"),
        P("col", "row"),
        P("col", None),
    )
    out_specs = P(("col", "depth"), "row")
    return jax.shard_map(
        per_device, mesh=mesh, in_specs=in_specs, out_specs=out_specs, check_vma=False
    )
```

profile of v0, /device:TPU:1, one launch (start us, length us, event | category | flops | bytes accessed | tf_op | source)
XLA Modules:
  0.0 242.5 jit_solution(16776493205895536926)
XLA Ops:
  6.5 0.0 copy-start
  6.5 0.0 copy-start.1
  6.5 0.0 all-gather.4.cloned.1.call-start
  6.5 0.7 convert_element_type.13
  7.3 0.1 broadcast_bitcast_fusion
  7.3 2.1 bitcast_multiply_fusion
  9.4 0.0 all-gather.4.cloned.1.call-update
  9.4 0.0 all-gather.6.cloned.1.call-start
  9.5 0.7 convert_bitcast_fusion
  10.2 0.1 broadcast_bitcast_fusion.2
  10.2 1.9 broadcast_multiply_fusion.1
  12.1 0.0 all-gather.6.cloned.1.call-update
  12.2 0.0 reduce-scatter.2.cloned.1.call-start
  12.2 0.0 copy-done
  12.2 0.0 copy-done.1
  12.3 0.1 broadcast_bitcast_fusion.1
  12.4 43.2 %all-gather.4.cloned.1.call-done = bf16[16,128,768]{2,1,0:T(8,128)(2,1)} async-done(((bf16[4,128,768]{2,1,0:T(8,128)(2,1)}), bf16[16,128,768]{2,1,0:T(8,128)(2,1)}) %all-gather.4.cloned.1.call-update) | async-done | bytes 3145744 | tf_op jit(solution)/shard_map/all_gather | solution.py:24
  55.5 71.2 %all-gather.6.cloned.1.call-done = bf16[16384,128]{1,0:T(8,128)(2,1)} async-done(((bf16[1024,128]{1,0:T(8,128)(2,1)}), bf16[16384,128]{1,0:T(8,128)(2,1)}) %all-gather.6.cloned.1.call-update) | async-done | bytes 4194320 | tf_op jit(solution)/shard_map/all_gather | solution.py:25
  126.7 6.2 %convolution_bitcast_fusion = f32[96,8,8,128]{3,1,2,0:T(8,128)S(1)} fusion(bf16[16,1024,128]{2,1,0:T(8,128)(2,1)} %bitcast.42, bf16[16,128,768]{2,1,0:T(8,128)(2,1)} %all-gather.4.cloned.1.call-done), kind=kOutput, calls=%fused_computation.2 | convolution fusion | flops 3221225472 | bytes 10485760 | tf_op jit(solution)/shard_map/sik,skn->in/dot_general | solution.py:26
  132.9 0.7 copy.22
  133.7 2.3 copy.15
  136.0 3.8 %broadcast_multiply_fusion = f32[8,128,6,128]{3,1,2,0:T(8,128)} fusion(f32[8,128,6,128]{3,1,2,0:T(8,128)} %copy.15, f32[8,6]{1,0:T(8,128)S(1)} %convert_element_type.14), kind=kLoop, calls=%fused_computation.3 | loop fusion | flops 786432 | bytes 6291648 | tf_op jit(solution)/shard_map/mul | solution.py:28
  139.8 2.6 %gather_fusion = f32[8,128,6,128]{3,1,2,0:T(8,128)S(1)} fusion(f32[8,128,6,128]{3,1,2,0:T(8,128)} %broadcast_multiply_fusion, s32[1024]{0:T(1024)S(1)} %pad_clamp_fusion), kind=kCustom, calls=%fused_computation | custom fusion | bytes 6291488 | tf_op jit(solution)/shard_map/jit(_take)/gather | solution.py:31
  142.5 2.4 copy.16
  144.9 4.3 %bitcast_select_fusion = f32[1024,768]{0,1:T(8,128)} fusion(f32[96,8,8,128]{3,2,1,0:T(8,128)} %bitcast.39, pred[1024]{0:T(1024)(128)(4,1)S(1)} %broadcast_bitcast_fusion.1), kind=kLoop, calls=%fused_computation.1 | loop fusion | flops 786432 | bytes 6292480 | tf_op jit(solution)/shard_map/jit(_take)/select_n | solution.py:31
  149.2 0.0 reduce-scatter.2.cloned.1.call-update
  149.2 84.9 %reduce-scatter.2.cloned.1.call-done = f32[128,768]{0,1:T(8,128)} async-done(((f32[1024,768]{0,1:T(8,128)}), f32[128,768]{0,1:T(8,128)}) %reduce-scatter.2.cloned.1.call-update) | async-done | bytes 393232 | tf_op jit(solution)/shard_map/reduce_scatter | solution.py:33
  234.1 1.0 convert_element_type.15
  235.1 0.8 copy.17
  (6 shorter events, 0.0 us)
Async XLA Ops:
  6.5 5.7 %copy-start = (s32[8,6]{1,0:T(8,128)S(1)}, s32[8,6]{1,0:T(8,128)}, u32[]{:S(2)}) copy-start(s32[8,6]{1,0:T(8,128)} %param.10) | copy-start | bytes 580
  6.5 5.7 %copy-start.1 = (s32[1,8]{1,0:T(1,128)S(1)}, s32[1,8]{1,0:T(1,128)}, u32[]{:S(2)}) copy-start(s32[1,8]{1,0:T(1,128)} %param.11) | copy-start | bytes 100
  6.5 49.0 %all-gather.4.cloned.1.call-start = ((), (), s32[]{:S(2)}) async-start(), calls=%async_computation.1 | async-start | bytes 3932160 | tf_op jit(solution)/shard_map/all_gather | solution.py:24
  9.4 117.3 %all-gather.6.cloned.1.call-start = ((), (), s32[]{:S(2)}) async-start(), calls=%async_computation.3 | async-start | bytes 4456448 | tf_op jit(solution)/shard_map/all_gather | solution.py:25
  12.2 221.9 %reduce-scatter.2.cloned.1.call-start = ((), (), s32[]{:S(2)}) async-start(), calls=%async_computation.2 | async-start | bytes 3538944 | tf_op jit(solution)/shard_map/reduce_scatter | solution.py:33
Sparse Core Ops, SparseCore 0:
  9.6 45.9 all-gather.3
  57.6 69.0 all-gather.5
  149.3 84.7 reduce-scatter.1
where the time goes:
time: 243 us; the launch traced here: 242 us
  waiting for transfers between devices  199 us (82%)
  other arithmetic  14.5 us (6%)
  between operations  13.2 us (5%)
  local copies, waits for them, and re-layouts  9.19 us (4%)
  matrix products  6.23 us (3%)
    reduce_scatter x1, waiting for transfers between devices, per_device(): lax.psum_scatter(arranged, 'depth', scatter_dimension=0, tiled=True)  84.9 us
    all_gather x1, waiting for transfers between devices, per_device(): ks_whole = lax.all_gather(ks_panel, 'row', axis=0, tiled=False)  71.2 us
    all_gather x1, waiting for transfers between devices, per_device(): sign_whole = lax.all_gather(sign_kept, 'col', axis=0, tiled=True)  43.2 us
    dot_general x1, matrix products, per_device(): jnp.einsum('sik,skn->in', ks_whole, sign_whole, preferred_element_type=jn...  6.23 us
    gather x2, local copies, waits for them, and re-layouts, per_device(): arranged = jnp.take(filtered, row_order[0], axis=0)  5.03 us
  transfers between devices with their start and end apart: 3, of which 3 were waited for; matrix products, arithmetic and copies ran while one was open for 1% of the time, Pallas kernels for 0%

commit v1 on v0

--- a/solution.py
+++ b/solution.py
@@ -21,7 +21,9 @@
         local_groups, sign_inner, 1, col_blocks, 1
     )
     sign_kept = sign_kept.reshape(local_groups, sign_inner * BS, col_blocks * BS)
-    sign_whole = lax.all_gather(sign_kept, "col", axis=0, tiled=True)
+    sign_whole = jnp.concatenate(
+        lax.all_to_all(jnp.stack([sign_kept] * lax.axis_size("col")), "col", 0, 0), axis=0
+    )
     ks_whole = lax.all_gather(ks_panel, "row", axis=0, tiled=False)
     product = jnp.einsum("sik,skn->in", ks_whole, sign_whole, preferred_element_type=jnp.float32)
     filtered = (

time: 243 us -> 195 us (0.80)
  waiting for transfers between devices: 199 us -> 142 us
  starting transfers between devices: 0.09 us -> 10.7 us
  other arithmetic: 14.5 us -> 9.76 us
  local copies, waits for them, and re-layouts: 9.19 us -> 11.9 us
    all_gather x1, waiting for transfers between devices: 71.2 us -> 19.7 us  [per_device(): ks_whole = lax.all_gather(ks_panel, 'row', axis=0, tiled=False)]
    all_gather x1 -> x0, waiting for transfers between devices: 43.2 us -> none  [per_device(): sign_whole = lax.all_gather(sign_kept, 'col', axis=0, tiled=True)]
    all_to_all x0 -> x1, waiting for transfers between devices: none -> 37.4 us  [per_device(): lax.all_to_all(jnp.stack([sign_kept] * lax.axis_size('col')), 'col', 0, 0)]
    all_to_all x0 -> x1, starting transfers between devices: none -> 10.7 us  [per_device(): lax.all_to_all(jnp.stack([sign_kept] * lax.axis_size('col')), 'col', 0, 0)]
    mul x1 -> x0, other arithmetic: 3.8 us -> none  [per_device(): product.reshape(row_blocks, BS, col_blocks, BS)]
    all_to_all x0 -> x1, local copies, waits for them, and re-layouts: none -> 2.75 us  [per_device(): lax.all_to_all(jnp.stack([sign_kept] * lax.axis_size('col')), 'col', 0, 0)]
    another operation x0 -> x1, local copies, waits for them, and re-layouts: none -> 2.48 us  [per_device(): jnp.stack([sign_kept] * lax.axis_size('col'))]
  transfers between devices with their start and end apart: 3 -> 3, of which waited for: 3 -> 3; matrix products, arithmetic and copies ran while one was open for 1% -> 4% of each run, Pallas kernels for 0% -> 0%
where the time goes in v1:
time: 195 us
  waiting for transfers between devices  142 us (73%)
  between operations  13.5 us (7%)
  local copies, waits for them, and re-layouts  11.9 us (6%)
  starting transfers between devices  10.7 us (5%)
  other arithmetic  9.76 us (5%)
  matrix products  7.39 us (4%)
    reduce_scatter x1, waiting for transfers between devices, per_device(): lax.psum_scatter(arranged, 'depth', scatter_dimension=0, tiled=True)  84.6 us
    all_to_all x1, waiting for transfers between devices, per_device(): lax.all_to_all(jnp.stack([sign_kept] * lax.axis_size('col')), 'col', 0, 0)  37.4 us
    all_gather x1, waiting for transfers between devices, per_device(): ks_whole = lax.all_gather(ks_panel, 'row', axis=0, tiled=False)  19.7 us
    all_to_all x1, starting transfers between devices, per_device(): lax.all_to_all(jnp.stack([sign_kept] * lax.axis_size('col')), 'col', 0, 0)  10.7 us
    dot_general x1, matrix products, per_device(): jnp.einsum('sik,skn->in', ks_whole, sign_whole, preferred_element_type=jn...  7.39 us
    gather x2, local copies, waits for them, and re-layouts, per_device(): arranged = jnp.take(filtered, row_order[0], axis=0)  5.02 us
    select_n x2, other arithmetic, per_device(): arranged = jnp.take(filtered, row_order[0], axis=0)  4.35 us
  transfers between devices with their start and end apart: 3, of which 3 were waited for; matrix products, arithmetic and copies ran while one was open for 4% of the time, Pallas kernels for 0%

profile of v1, /device:TPU:1, one launch (start us, length us, event | category | flops | bytes accessed | tf_op | source)
XLA Modules:
  0.0 195.0 jit_solution(847398949806964526)
XLA Ops:
  6.5 0.0 all-gather.3.cloned.1.call-start
  6.5 0.7 convert_bitcast_fusion
  7.2 0.1 broadcast_bitcast_fusion.2
  7.3 1.8 broadcast_multiply_fusion
  9.1 0.0 all-gather.3.cloned.1.call-update
  9.1 0.7 convert_element_type.13
  9.8 0.1 broadcast_bitcast_fusion
  9.9 1.2 bitcast_multiply_fusion.1
  11.1 0.6 copy.19
  11.7 2.5 %stack.3 = bf16[4,4,128,768]{2,1,3,0:T(4,128)(2,1)} broadcast(bf16[4,128,768]{1,0,2:T(4,128)(2,1)S(1)} %copy.19), dimensions={1,2,3} | broadcast | bytes 3932160 | tf_op jit(solution)/shard_map/stack | solution.py:25
  14.2 0.0 copy-start
  14.2 0.0 copy-start.1
  14.2 10.7 %all-to-all-start = ((bf16[4,4,128,768]{2,1,3,0:T(4,128)(2,1)}), bf16[4,4,128,768]{2,1,3,0:T(4,128)(2,1)S(1)}, u32[]{:S(2)}, u32[]{:S(2)}) async-start(bf16[4,4,128,768]{2,1,3,0:T(4,128)(2,1)} %stack.3), calls=%async_computation | async-start | bytes 6291456 | tf_op jit(solution)/shard_map/all_to_all | solution.py:25
  24.9 0.0 reduce-scatter.2.cloned.1.call-start
  24.9 0.0 copy-done
  24.9 0.0 copy-done.1
  24.9 0.1 broadcast_bitcast_fusion.1
  25.0 37.4 %all-to-all-done = bf16[4,4,128,768]{2,1,3,0:T(4,128)(2,1)S(1)} async-done(((bf16[4,4,128,768]{2,1,3,0:T(4,128)(2,1)}), bf16[4,4,128,768]{2,1,3,0:T(4,128)(2,1)S(1)}, u32[]{:S(2)}, u32[]{:S(2)}) %all-to-all-start) | async-done | bytes 3145760 | tf_op jit(solution)/shard_map/all_to_all | solution.py:25
  62.5 2.8 %copy.20 = bf16[4,4,128,768]{2,1,0,3:T(4,128)(2,1)} copy(bf16[4,4,128,768]{2,1,3,0:T(4,128)(2,1)S(1)} %all-to-all-done) | data formatting | bytes 6291456 | tf_op jit(solution)/shard_map/all_to_all | solution.py:25
  65.2 19.7 %all-gather.3.cloned.1.call-done = bf16[16384,128]{1,0:T(8,128)(2,1)} async-done(((bf16[1024,128]{1,0:T(8,128)(2,1)}), bf16[16384,128]{1,0:T(8,128)(2,1)}) %all-gather.3.cloned.1.call-update) | async-done | bytes 4194320 | tf_op jit(solution)/shard_map/all_gather | solution.py:27
  84.9 7.4 %bitcast_multiply_fusion = f32[8,128,6,128]{3,1,2,0:T(8,128)} fusion(bf16[6,128,128,16]{2,3,1,0:T(8,128)(2,1)} %bitcast.49, bf16[8,128,128,16,1]{2,1,0,3,4:T(8,128)(2,1)} %bitcast.52, f32[8,6]{1,0:T(8,128)S(1)} %convert_element_type.14), kind=kOutput, calls=%fused_computation.4 | convolution fusion | flops 3222011904 | bytes 10485952 | tf_op jit(solution)/shard_map/sik,skn->in/dot_general | solution.py:28
  92.3 2.6 %gather_fusion = f32[8,128,6,128]{3,1,2,0:T(8,128)S(1)} fusion(f32[8,128,6,128]{3,1,2,0:T(8,128)} %bitcast_multiply_fusion, s32[1024]{0:T(1024)S(1)} %pad_clamp_fusion), kind=kCustom, calls=%fused_computation | custom fusion | bytes 6291488 | tf_op jit(solution)/shard_map/jit(_take)/gather | solution.py:33
  95.0 2.4 %copy.23 = f32[8,128,6,128]{1,0,3,2:T(8,128)} copy(f32[8,128,6,128]{3,1,2,0:T(8,128)S(1)} %gather_fusion) | data formatting | bytes 6291456 | tf_op jit(solution)/shard_map/jit(_take)/gather | solution.py:33
  97.4 4.3 %bitcast_select_fusion = f32[1024,768]{0,1:T(8,128)} fusion(f32[96,8,8,128]{3,2,1,0:T(8,128)} %bitcast.48, pred[1024]{0:T(1024)(128)(4,1)S(1)} %broadcast_bitcast_fusion.1), kind=kLoop, calls=%fused_computation.3 | loop fusion | flops 786432 | bytes 6292480 | tf_op jit(solution)/shard_map/jit(_take)/select_n | solution.py:33
  101.7 0.0 reduce-scatter.2.cloned.1.call-update
  101.7 84.6 %reduce-scatter.2.cloned.1.call-done = f32[128,768]{0,1:T(8,128)} async-done(((f32[1024,768]{0,1:T(8,128)}), f32[128,768]{0,1:T(8,128)}) %reduce-scatter.2.cloned.1.call-update) | async-done | bytes 393232 | tf_op jit(solution)/shard_map/reduce_scatter | solution.py:35
  186.3 1.0 convert_element_type.15
  187.4 0.8 copy.24
  (6 shorter events, 0.0 us)
Async XLA Ops:
  6.5 78.4 %all-gather.3.cloned.1.call-start = ((), (), s32[]{:S(2)}) async-start(), calls=%async_computation.3 | async-start | bytes 4456448 | tf_op jit(solution)/shard_map/all_gather | solution.py:27
  14.2 10.7 %copy-start = (s32[8,6]{1,0:T(8,128)S(1)}, s32[8,6]{1,0:T(8,128)}, u32[]{:S(2)}) copy-start(s32[8,6]{1,0:T(8,128)} %param.10) | copy-start | bytes 580
  14.2 10.7 %copy-start.1 = (s32[1,8]{1,0:T(1,128)S(1)}, s32[1,8]{1,0:T(1,128)}, u32[]{:S(2)}) copy-start(s32[1,8]{1,0:T(1,128)} %param.11) | copy-start | bytes 100
  14.2 48.2 %all-to-all-start = ((bf16[4,4,128,768]{2,1,3,0:T(4,128)(2,1)}), bf16[4,4,128,768]{2,1,3,0:T(4,128)(2,1)S(1)}, u32[]{:S(2)}, u32[]{:S(2)}) async-start(bf16[4,4,128,768]{2,1,3,0:T(4,128)(2,1)} %stack.3), calls=%async_computation | async-start | bytes 6291456 | tf_op jit(solution)/shard_map/all_to_all | solution.py:25
  24.9 161.5 %reduce-scatter.2.cloned.1.call-start = ((), (), s32[]{:S(2)}) async-start(), calls=%async_computation.2 | async-start | bytes 3538944 | tf_op jit(solution)/shard_map/reduce_scatter | solution.py:35
Sparse Core Ops, SparseCore 0:
  9.4 75.4 all-gather.2
  101.8 84.4 reduce-scatter.1
